TPU v7x, 256 devices: a whole 4x4x8 slice. The times are simulated.
256 devices in a mesh: row: 8 (over y, core), col: 32 (over x, z).
Axes of the slice: x: 4, y: 4, z: 8, core: 2. Of those that a mesh axis runs over, the one named last changes fastest.
Arguments:
- hidden: bfloat16 [32768, 4608], P('col', 'row'), may hold values from -6 to 6
- w_query: bfloat16 [4608, 4096], P('col', 'row'), may hold values from -0.09375 to 0.09375
- w_key: bfloat16 [4608, 2048], P('col', 'row'), may hold values from -0.09375 to 0.09375
- w_value: bfloat16 [4608, 2048], P('col', 'row'), may hold values from -0.09375 to 0.09375
- adapter_down: bfloat16 [32, 4608, 32], P('col', 'row'), may hold values from -0.09375 to 0.09375
- adapter_up_query: bfloat16 [32, 16, 4096], P('col', None, 'row'), may hold values from -1.5 to 1.5
- adapter_up_value: bfloat16 [32, 16, 2048], P('col', None, 'row'), may hold values from -1.5 to 1.5
- lengths: int32 [32, 10], P('col'), may hold values from 1 to 192, 1024 in all within a row
- request_adapter: int32 [32, 10], P('col'), may hold values from 0 to 31
- adapter_slot: int32 [32], replicated, may hold values from 0 to 31, each once
- page_table: int32 [32, 18], P('col'), may hold values from 0 to 17, each once within a row
Outputs:
- query: bfloat16 [32768, 4096], P('col', 'row')
- key_cache: bfloat16 [576, 128, 2048], P('col', None, 'row')
- value_cache: bfloat16 [576, 128, 2048], P('col', None, 'row')
Inputs may be any that keep to these rules, and one draw needn't show every extreme that they name: Each row of lengths sums to 1024, and its longest request has exactly 192 tokens. `adapter_slot`: a permutation of the slots. `page_table`: each row is a permutation of the 18 local slots.
All inputs are finite; a program needn't handle non-finite values.
Results may differ from a plain program's by a relative error of at most 0.0039.
Values may be sent and summed in bfloat16 or wider, within the bound.
No kernel may reach another device: no remote copies, remote signals or barrier semaphores. Data moves between devices by JAX's collectives and lax.ppermute only.
A program may use at most 128 MiB of HBM per device.

v0:
```python
import math
import jax
import jax.numpy as jnp
from jax import lax
from jax.sharding import PartitionSpec as P

HEAD = 128
PAGE = 128
MOST = 192
TOK_DEV = 1024


def rotate(values, position):
    half_width = HEAD // 2
    frequency = jnp.exp(
        jnp.arange(half_width, dtype=jnp.float32) * (-2.0 * math.log(10000.0) / HEAD)
    )
    angles = position.astype(jnp.float32)[:, None] * frequency[None, :]
    cosine = jnp.cos(angles)[:, None, :]
    sine_value = jnp.sin(angles)[:, None, :]
    shaped = values.reshape(values.shape[0], -1, HEAD)
    leading = shaped[:, :, :half_width]
    second = shaped[:, :, half_width:]
    rotated = jnp.concatenate(
        [leading * cosine - second * sine_value, second * cosine + leading * sine_value], axis=2
    )
    return rotated.reshape(values.shape)


def layout(lengths, page_row):
    token_index = jnp.arange(TOK_DEV, dtype=jnp.int32)
    starts = jnp.cumsum(lengths) - lengths
    request_of = jnp.sum((token_index[:, None] >= starts[None, :]).astype(jnp.int32), axis=1) - 1
    position = token_index - jnp.take(starts, request_of)
    pages_each = (lengths + PAGE - 1) // PAGE
    page_start = jnp.cumsum(pages_each) - pages_each
    page_index = jnp.take(page_start, request_of) + position // PAGE
    target = jnp.take(page_row, page_index) * PAGE + position % PAGE
    return (starts, request_of, position, target)


def expand_up(lowrank, chosen, up_query, up_value):
    adapter_count = up_query.shape[0]
    rank_width = up_query.shape[1]
    onehot = (chosen[:, None] == jnp.arange(adapter_count, dtype=jnp.int32)[None, :]).astype(
        lowrank.dtype
    )
    spread_query = (onehot[:, :, None] * lowrank[:, None, :rank_width]).reshape(
        -1, adapter_count * rank_width
    )
    spread_value = (onehot[:, :, None] * lowrank[:, None, rank_width:]).reshape(
        -1, adapter_count * rank_width
    )
    delta_query = jnp.dot(
        spread_query,
        up_query.reshape(adapter_count * rank_width, -1),
        preferred_element_type=jnp.float32,
    )
    delta_value = jnp.dot(
        spread_value,
        up_value.reshape(adapter_count * rank_width, -1),
        preferred_element_type=jnp.float32,
    )
    return (delta_query, delta_value)


def project_down(source, down_all, starts, lengths, chosen_request):
    tokens = source.shape[0]
    padded = jnp.concatenate([source, jnp.zeros((MOST, source.shape[1]), source.dtype)], axis=0)
    result = jnp.zeros((tokens + MOST, down_all.shape[2]), jnp.float32)
    inner_rows = jnp.arange(MOST, dtype=jnp.int32)

    def one_request(number, result):
        first_row = starts[number]
        window = lax.dynamic_slice_in_dim(padded, first_row, MOST, 0)
        factor = lax.dynamic_index_in_dim(down_all, chosen_request[number], 0, keepdims=False)
        partial_sum = jnp.dot(window, factor, preferred_element_type=jnp.float32)
        inside = (inner_rows < lengths[number]).astype(jnp.float32)[:, None]
        current = lax.dynamic_slice_in_dim(result, first_row, MOST, 0)
        return lax.dynamic_update_slice_in_dim(result, current + partial_sum * inside, first_row, 0)

    result = lax.fori_loop(0, starts.shape[0], one_request, result)
    return result[:tokens]


def shards(
    hidden,
    w_query,
    w_key,
    w_value,
    adapter_down,
    adapter_up_query,
    adapter_up_value,
    lengths,
    request_adapter,
    adapter_slot,
    page_table,
):
    starts, request_of, position, target = layout(lengths[0], page_table[0])
    full_rows = lax.all_gather(hidden, "row", axis=1, tiled=True)
    base_query = jnp.dot(
        full_rows,
        lax.all_gather(w_query, "col", axis=0, tiled=True),
        preferred_element_type=jnp.float32,
    )
    base_key = jnp.dot(
        full_rows,
        lax.all_gather(w_key, "col", axis=0, tiled=True),
        preferred_element_type=jnp.float32,
    )
    base_value = jnp.dot(
        full_rows,
        lax.all_gather(w_value, "col", axis=0, tiled=True),
        preferred_element_type=jnp.float32,
    )
    up_query, up_value = (
        lax.all_gather(adapter_up_query, "col", axis=0, tiled=True),
        lax.all_gather(adapter_up_value, "col", axis=0, tiled=True),
    )
    chosen_request = jnp.take(adapter_slot, request_adapter[0])
    rows_all = lax.all_gather(adapter_down, "row", axis=1, tiled=True)
    down_all = lax.all_gather(rows_all, "col", axis=0, tiled=True)
    lowrank = project_down(full_rows, down_all, starts, lengths[0], chosen_request)
    lowrank = lowrank.astype(jnp.bfloat16)
    chosen = jnp.take(chosen_request, request_of)
    delta_query, delta_value = expand_up(lowrank, chosen, up_query, up_value)
    query = rotate(base_query + delta_query, position).astype(jnp.bfloat16)
    key_rotated = rotate(base_key, position).astype(jnp.bfloat16)
    value_rows = (base_value + delta_value).astype(jnp.bfloat16)
    pages = page_table.shape[1]
    key_width = w_key.shape[1]
    key_cache = (
        jnp.zeros((pages * PAGE, key_width), jnp.bfloat16)
        .at[target]
        .set(key_rotated)
        .reshape(pages, PAGE, key_width)
    )
    value_cache = (
        jnp.zeros((pages * PAGE, key_width), jnp.bfloat16)
        .at[target]
        .set(value_rows)
        .reshape(pages, PAGE, key_width)
    )
    return (query, key_cache, value_cache)


def solution(mesh):
    return jax.shard_map(
        shards,
        mesh=mesh,
        in_specs=(
            P("col", "row"),
            P("col", "row"),
            P("col", "row"),
            P("col", "row"),
            P("col", "row", None),
            P("col", None, "row"),
            P("col", None, "row"),
            P("col", None),
            P("col", None),
            P(),
            P("col", None),
        ),
        out_specs=(P("col", "row"), P("col", None, "row"), P("col", None, "row")),
        check_vma=False,
    )
```

profile of v0, /device:TPU:1, one launch (start us, length us, event | category | flops | bytes accessed | tf_op | source)
XLA Modules:
  0.0 450.9 jit_solution(18159563451350654746)
XLA Ops:
  10.4 18.8 %all_gather.26 = bf16[1,4608,32]{2,0,1:T(2,128)(2,1)S(1)} all-gather(bf16[1,576,32]{2,0,1:T(2,128)(2,1)S(1)} %copy.40), channel_id=1, replica_groups=mesh['row'=8,'col'=32] {'row'}, dimensions={1}, use_global_device_ids=true | all-gather | bytes 331776 | tf_op jit(solution)/shard_map/all_gather | solution.py:121
  29.3 3.7 copy.41
  37.6 24.0 %compare_select_fusion.1 = (s32[1024]{0:T(1024)S(1)}, pred[1024]{0:T(1024)(128)(4,1)S(1)}, pred[1024]{0:T(1024)(128)(4,1)S(1)}, pred[1024]{0:T(1024)(128)(4,1)S(...) fusion(s32[]{:T(128)} %bitcast.41, s32[]{:T(128)} %bitcast.40, ...), kind=kLoop, calls=%fused_computation.41 | loop fusion | flops 105472 | bytes 18584 | tf_op jit(solution)/shard_map/select_n | solution.py:135
  61.6 6.4 %fusion.31 = f32[1024]{0:T(1024)S(1)} fusion(pred[1024]{0:T(1024)(128)(4,1)S(1)} %get-tuple-element.205, pred[1024]{0:T(1024)(128)(4,1)S(1)} %get-tuple-element.204, pred[1024]{0:T(1024)(128)(4,1)S(1)} %get-tuple-element.203, pred[1024]{0:T(1024)(128)(4,1)S(1)} %get-tuple-element.202, pred[1024]{0:T(1024)(128)(4,1)S(1)} %get-tuple-element.201, ...), kind=kLoop, calls=%fused_computation.58 | loop fusion | flops 12288 | bytes 14376 | tf_op jit(solution)/shard_map/convert_element_type | solution.py:18
  68.0 6.3 %select_select_fusion = s32[1024]{0:T(1024)S(1)} fusion(pred[1024]{0:T(1024)(128)(4,1)S(1)} %get-tuple-element.205, pred[1024]{0:T(1024)(128)(4,1)S(1)} %get-tuple-element.204, pred[1024]{0:T(1024)(128)(4,1)S(1)} %get-tuple-element.203, pred[1024]{0:T(1024)(128)(4,1)S(1)} %get-tuple-element.202, pred[1024]{0:T(1024)(128)(4,1)S(1)} %get-tuple-element.201, ...), kind=kLoop, calls=%fused_computation.52 | loop fusion | flops 10240 | bytes 14376 | tf_op jit(solution)/shard_map/jit(_take)/select_n | solution.py:125
  74.3 42.7 %all_gather.28 = bf16[32,16,512]{2,1,0:T(8,128)(2,1)S(1)} all-gather(bf16[1,16,512]{2,1,0:T(8,128)(2,1)S(1)} %copy-done.4), channel_id=1, replica_groups=mesh['row'=8,'col'=32] {'col'}, dimensions={0}, use_global_device_ids=true | all-gather | bytes 540672 | tf_op jit(solution)/shard_map/all_gather | solution.py:117
  117.1 43.2 %all_gather.31 = bf16[32,16,256]{2,1,0:T(8,128)(2,1)} all-gather(bf16[1,16,256]{2,1,0:T(8,128)(2,1)S(1)} %copy-done.5), channel_id=1, replica_groups=mesh['row'=8,'col'=32] {'col'}, dimensions={0}, use_global_device_ids=true | all-gather | bytes 270336 | tf_op jit(solution)/shard_map/all_gather | solution.py:118
  161.3 6.1 %fusion.40 = f32[1024,256]{0,1:T(8,128)S(1)} fusion(bf16[1024,4608]{0,1:T(8,128)(2,1)} %all-gather.6.cloned.1.call-done, bf16[4608,256]{1,0:T(8,128)(2,1)} %all-gather.12.cloned.1.call-done), kind=kOutput, calls=%fused_computation.91 | convolution fusion | flops 2415919104 | bytes 12845056 | tf_op jit(solution)/shard_map/dot_general | solution.py:106
  167.8 12.7 %copy.51 = bf16[1024,4608]{1,0:T(8,128)(2,1)} copy(bf16[1024,4608]{0,1:T(8,128)(2,1)} %all-gather.6.cloned.1.call-done) | data formatting | bytes 18874368
  180.6 9.1 %concatenate.11.clone = bf16[1216,4608]{1,0:T(8,128)(2,1)} pad(bf16[1024,4608]{1,0:T(8,128)(2,1)} %copy.51, bf16[]{:T(256)} %constant.127.clone.1), padding=0_192x0_0 | pad | bytes 20643842 | tf_op jit(solution)/shard_map/concatenate | solution.py:69
  189.6 6.1 %scatter_custom_fusion = bf16[2304,256]{1,0:T(8,128)(2,1)} fusion(s32[1024]{0:T(1024)S(1)} %get-tuple-element.195, bf16[1024,256]{1,0:T(8,128)(2,1)S(1)} %copy.49, bf16[]{:T(256)} %constant.127.clone.1), kind=kCustom, calls=%fused_computation.23 | custom fusion | bytes 1179650 | tf_op jit(solution)/shard_map/scatter | solution.py:135
  195.7 34.8 %all-gather.8.cloned.1.call-done = bf16[4608,512]{1,0:T(8,128)(2,1)} async-done(((bf16[144,512]{1,0:T(8,128)(2,1)}), bf16[4608,512]{1,0:T(8,128)(2,1)}) %all-gather.8.cloned.1.call-update) | async-done | bytes 4718608 | tf_op jit(solution)/shard_map/all_gather | solution.py:103
  230.6 9.1 %fusion.39 = f32[1024,512]{0,1:T(8,128)S(1)} fusion(bf16[1024,4608]{0,1:T(8,128)(2,1)} %all-gather.6.cloned.1.call-done, bf16[4608,512]{1,0:T(8,128)(2,1)} %all-gather.8.cloned.1.call-done), kind=kOutput, calls=%fused_computation.90 | convolution fusion | flops 4831838208 | bytes 16252928 | tf_op jit(solution)/shard_map/dot_general | solution.py:101
  239.7 97.2 %all-gather.10.cloned.1.call-done = bf16[32,4608,32]{1,2,0:T(8,128)(2,1)} async-done(((bf16[1,4608,32]{1,2,0:T(8,128)(2,1)}), bf16[32,4608,32]{1,2,0:T(8,128)(2,1)}) %all-gather.10.cloned.1.call-update) | async-done | bytes 9437200 | tf_op jit(solution)/shard_map/all_gather | solution.py:122
  336.9 91.2 %while.14 = (s32[]{:T(128)}, f32[1216,32]{0,1:T(8,128)S(1)}, s32[10]{0:T(128)S(1)}, bf16[1216,4608]{1,0:T(8,128)(2,1)}, s32[10]{0:T(128)S(1)}, /*index=5*/bf16[3...) while((s32[]{:T(128)}, f32[1216,32]{0,1:T(8,128)S(1)}, ...), condition=%wide.region_3.5_spmd.clone, body=%wide.region_2.4_spmd.clone.sunk | while | flops 56635784 | bytes 2165981 | solution.py:82
  343.2 2.2 fusion.52
  352.2 2.2 fusion.52
  361.3 2.2 fusion.52
  370.5 2.2 fusion.52
  397.9 2.2 fusion.52
  407.0 2.2 fusion.52
  425.3 2.2 fusion.52
  431.3 7.0 %fusion.13 = bf16[1024,256]{1,0:T(8,128)(2,1)S(1)} fusion(f32[1024,256]{1,0:T(8,128)S(1)} %convolution_bitcast_fusion, bf16[1024,4608]{0,1:T(8,128)(2,1)} %all-gather.6.cloned.1.call-done, bf16[4608,256]{1,0:T(8,128)(2,1)} %all-gather.14.cloned.1.call-done), kind=kOutput, calls=%fused_computation.15 | convolution fusion | flops 2416443392 | bytes 13369344 | tf_op jit(solution)/shard_map/dot_general | solution.py:111
  438.3 6.1 %scatter_custom_fusion.1 = bf16[2304,256]{1,0:T(8,128)(2,1)} fusion(s32[1024]{0:T(1024)S(1)} %get-tuple-element.195, bf16[1024,256]{1,0:T(8,128)(2,1)S(1)} %fusion.13, bf16[]{:T(256)} %constant.127.clone.1), kind=kCustom, calls=%fused_computation.21 | custom fusion | bytes 1179650 | tf_op jit(solution)/shard_map/scatter | solution.py:141
  (110 shorter events, 48.8 us)
Async XLA Ops:
  7.2 27.6 %copy-start = (s32[32]{0:T(128)S(1)}, s32[32]{0:T(128)}, u32[]{:S(2)}) copy-start(s32[32]{0:T(128)} %param.24) | copy-start | bytes 388
  7.2 154.1 %all-gather.12.cloned.1.call-start = ((), (), s32[]{:S(2)}) async-start(), calls=%async_computation.3 | async-start | bytes 2433024 | tf_op jit(solution)/shard_map/all_gather | solution.py:108
  7.9 153.4 %all-gather.6.cloned.1.call-start = ((), (), s32[]{:S(2)}) async-start(), calls=%async_computation | async-start | bytes 10616832 | tf_op jit(solution)/shard_map/all_gather | solution.py:100
  8.7 221.9 %all-gather.8.cloned.1.call-start = ((), (), s32[]{:S(2)}) async-start(), calls=%async_computation.1 | async-start | bytes 4866048 | tf_op jit(solution)/shard_map/all_gather | solution.py:103
  9.4 327.5 %all-gather.10.cloned.1.call-start = ((), (), s32[]{:S(2)}) async-start(), calls=%async_computation.2 | async-start | bytes 9732096 | tf_op jit(solution)/shard_map/all_gather | solution.py:122
  10.4 23.2 %copy-start.3 = (s32[1,18]{1,0:T(1,128)S(1)}, s32[1,18]{1,0:T(1,128)}, u32[]{:S(2)}) copy-start(s32[1,18]{1,0:T(1,128)} %param.25) | copy-start | bytes 220
  10.4 23.9 %copy-start.7 = (s32[1,10]{1,0:T(1,128)S(1)}, s32[1,10]{1,0:T(1,128)}, u32[]{:S(2)}) copy-start(s32[1,10]{1,0:T(1,128)} %param.22) | copy-start | bytes 124
  10.4 24.1 %copy-start.6 = (s32[1,10]{1,0:T(1,128)S(1)}, s32[1,10]{1,0:T(1,128)}, u32[]{:S(2)}) copy-start(s32[1,10]{1,0:T(1,128)} %param.23) | copy-start | bytes 124
  29.3 45.1 %copy-start.4 = (bf16[1,16,512]{2,1,0:T(8,128)(2,1)S(1)}, bf16[1,16,512]{2,1,0:T(8,128)(2,1)}, u32[]{:S(2)}) copy-start(bf16[1,16,512]{2,1,0:T(8,128)(2,1)} %param.20) | copy-start | bytes 49156
  29.3 87.8 %copy-start.5 = (bf16[1,16,256]{2,1,0:T(8,128)(2,1)S(1)}, bf16[1,16,256]{2,1,0:T(8,128)(2,1)}, u32[]{:S(2)}) copy-start(bf16[1,16,256]{2,1,0:T(8,128)(2,1)} %param.21) | copy-start | bytes 24580
  33.0 398.3 %all-gather.14.cloned.1.call-start = ((), (), s32[]{:S(2)}) async-start(), calls=%async_computation.4 | async-start | bytes 2433024 | tf_op jit(solution)/shard_map/all_gather | solution.py:113
  429.3 1.4 copy-start.2
  431.3 13.1 %copy-start.1 = (s32[32]{0:T(128)S(1)}, s32[32]{0:T(128)}, u32[]{:S(2)}) copy-start(s32[32]{0:T(128)} %param.24) | copy-start | bytes 388
Sparse Core Ops, SparseCore 0:
  10.6 77.8 all-gather.11
  90.3 58.5 all-gather.5
  151.5 79.0 all-gather.7
  233.6 103.2 all-gather.9
  339.3 71.4 all-gather.13
where the time goes:
time: 453 us; the launch traced here: 451 us
  waiting for transfers between devices  135 us (30%)
  blocking collectives  105 us (23%)
  local copies, waits for them, and re-layouts  67.1 us (15%)
  matrix products  45.5 us (10%)
  other arithmetic  45.3 us (10%)
  loops' own time  39.3 us (9%)
  between operations  14.1 us (3%)
    all_gather x1, waiting for transfers between devices, shards(): down_all = lax.all_gather(rows_all, 'col', axis=0, tiled=True)  97.2 us
    all_gather x1, blocking collectives, shards(): lax.all_gather(adapter_up_value, 'col', axis=0, tiled=True)  43.2 us
    all_gather x1, blocking collectives, shards(): lax.all_gather(adapter_up_query, 'col', axis=0, tiled=True)  42.7 us
    another operation x1, loops' own time, project_down(): result = lax.fori_loop(0, starts.shape[0], one_request, result)  39.3 us
    all_gather x1, waiting for transfers between devices, shards(): lax.all_gather(w_query, 'col', axis=0, tiled=True)  34.8 us
    select_n x1, other arithmetic, shards(): key_cache = jnp.zeros((pages * PAGE, key_width), jnp.bfloat16).at[target]...  24 us
    dot_general x10, matrix products, one_request(): partial_sum = jnp.dot(window, factor, preferred_element_type=jnp.float32)  22 us
    all_gather x1, blocking collectives, shards(): rows_all = lax.all_gather(adapter_down, 'row', axis=1, tiled=True)  18.8 us
  transfers between devices with their start and end apart: 5, of which 2 were waited for; matrix products, arithmetic and copies ran while one was open for 32% of the time, Pallas kernels for 0%

commit v1 on v0

--- a/solution.py
+++ b/solution.py
@@ -118,7 +118,25 @@
         lax.all_gather(adapter_up_value, "col", axis=0, tiled=True),
     )
     chosen_request = jnp.take(adapter_slot, request_adapter[0])
-    rows_all = lax.all_gather(adapter_down, "row", axis=1, tiled=True)
+    heard, all_rows, u1 = (lax.axis_size("row"), lax.axis_index("row"), adapter_down.shape[1])
+    leaves = [(i, (i + 1) % heard) for i in range(heard)]
+    grid = [(i, (i - 1) % heard) for i in range(heard)]
+    rows_all = jnp.zeros(
+        (*adapter_down.shape[:1], heard * u1, *adapter_down.shape[2:]), adapter_down.dtype
+    )
+    rows_all = lax.dynamic_update_slice_in_dim(rows_all, adapter_down, all_rows * u1, axis=1)
+    new = near = adapter_down
+    outcome_arr = heard // 2
+    for q in tuple(range(1, outcome_arr + 1)):
+        new = lax.ppermute(new, "row", leaves)
+        rows_all = lax.dynamic_update_slice_in_dim(
+            rows_all, new, (all_rows - q) % heard * u1, axis=1
+        )
+        if q < heard - outcome_arr:
+            near = lax.ppermute(near, "row", grid)
+            rows_all = lax.dynamic_update_slice_in_dim(
+                rows_all, near, (all_rows + q) % heard * u1, axis=1
+            )
     down_all = lax.all_gather(rows_all, "col", axis=0, tiled=True)
     lowrank = project_down(full_rows, down_all, starts, lengths[0], chosen_request)
     lowrank = lowrank.astype(jnp.bfloat16)

time: 453 us -> 453 us (level)
  blocking collectives: 105 us -> 86.8 us
  starting transfers between devices: 0.19 us -> 11.4 us
  waiting for transfers between devices: 135 us -> 140 us
    all_gather x1 -> x0, blocking collectives: 18.8 us -> none  [shards(): rows_all = lax.all_gather(adapter_down, 'row', axis=1, tiled=True)]
    ppermute x0 -> x7, starting transfers between devices: none -> 11.2 us  [the longest x4 5.85 us: shards(): new = lax.ppermute(new, 'row', leaves)]
    dynamic_update_slice x0 -> x8, local copies, waits for them, and re-layouts: none -> 5.24 us  [the longest x4 2.22 us: shards(): lax.dynamic_update_slice_in_dim(rows_all, new, (all_rows - q) % heard * u...]
    unnamed x18 -> x17, local copies, waits for them, and re-layouts: 13.7 us -> 13.5 us
  transfers between devices with their start and end apart: 5 -> 12, of which waited for: 2 -> 5; matrix products, arithmetic and copies ran while one was open for 32% -> 32% of each run, Pallas kernels for 0% -> 0%
where the time goes in v1:
time: 453 us; the launch traced here: 451 us
  waiting for transfers between devices  140 us (31%)
  blocking collectives  86.8 us (19%)
  local copies, waits for them, and re-layouts  68.6 us (15%)
  matrix products  45.5 us (10%)
  other arithmetic  45.4 us (10%)
  loops' own time  39.3 us (9%)
  between operations  14.2 us (3%)
  starting transfers between devices  11.4 us (3%)
    all_gather x1, waiting for transfers between devices, shards(): down_all = lax.all_gather(rows_all, 'col', axis=0, tiled=True)  97.2 us
    all_gather x1, blocking collectives, shards(): lax.all_gather(adapter_up_query, 'col', axis=0, tiled=True)  44.3 us
    all_gather x1, blocking collectives, shards(): lax.all_gather(adapter_up_value, 'col', axis=0, tiled=True)  42.5 us
    another operation x1, loops' own time, project_down(): result = lax.fori_loop(0, starts.shape[0], one_request, result)  39.3 us
    all_gather x1, waiting for transfers between devices, shards(): lax.all_gather(w_query, 'col', axis=0, tiled=True)  37.9 us
    select_n x1, other arithmetic, shards(): key_cache = jnp.zeros((pages * PAGE, key_width), jnp.bfloat16).at[target]...  24.2 us
    dot_general x10, matrix products, one_request(): partial_sum = jnp.dot(window, factor, preferred_element_type=jnp.float32)  22 us
    unnamed x17, local copies, waits for them, and re-layouts  13.5 us
  transfers between devices with their start and end apart: 12, of which 5 were waited for; matrix products, arithmetic and copies ran while one was open for 32% of the time, Pallas kernels for 0%

profile of v1, /device:TPU:1, one launch (start us, length us, event | category | flops | bytes accessed | tf_op | source)
XLA Modules:
  0.0 451.1 jit_solution(13747035122756696652)
XLA Ops:
  9.5 2.7 collective-permute-start
  19.3 3.0 collective-permute-start.5
  29.7 44.3 %all_gather.24 = bf16[32,16,512]{2,1,0:T(8,128)(2,1)S(1)} all-gather(bf16[1,16,512]{2,1,0:T(8,128)(2,1)S(1)} %copy-done.4), channel_id=1, replica_groups=mesh['row'=8,'col'=32] {'col'}, dimensions={0}, use_global_device_ids=true | all-gather | bytes 540672 | tf_op jit(solution)/shard_map/all_gather | solution.py:117
  78.0 24.2 %compare_select_fusion.1 = (s32[1024]{0:T(1024)S(1)}, pred[1024]{0:T(1024)(128)(4,1)S(1)}, pred[1024]{0:T(1024)(128)(4,1)S(1)}, pred[1024]{0:T(1024)(128)(4,1)S(...) fusion(s32[]{:T(128)} %bitcast.41, s32[]{:T(128)} %bitcast.40, ...), kind=kLoop, calls=%fused_computation.41 | loop fusion | flops 105472 | bytes 18584 | tf_op jit(solution)/shard_map/select_n | solution.py:153
  102.3 6.4 %fusion.31 = f32[1024]{0:T(1024)S(1)} fusion(pred[1024]{0:T(1024)(128)(4,1)S(1)} %get-tuple-element.198, pred[1024]{0:T(1024)(128)(4,1)S(1)} %get-tuple-element.197, pred[1024]{0:T(1024)(128)(4,1)S(1)} %get-tuple-element.196, pred[1024]{0:T(1024)(128)(4,1)S(1)} %get-tuple-element.195, pred[1024]{0:T(1024)(128)(4,1)S(1)} %get-tuple-element.194, ...), kind=kLoop, calls=%fused_computation.58 | loop fusion | flops 12288 | bytes 14376 | tf_op jit(solution)/shard_map/convert_element_type | solution.py:18
  108.7 6.1 %select_select_fusion = s32[1024]{0:T(1024)S(1)} fusion(pred[1024]{0:T(1024)(128)(4,1)S(1)} %get-tuple-element.198, pred[1024]{0:T(1024)(128)(4,1)S(1)} %get-tuple-element.197, pred[1024]{0:T(1024)(128)(4,1)S(1)} %get-tuple-element.196, pred[1024]{0:T(1024)(128)(4,1)S(1)} %get-tuple-element.195, pred[1024]{0:T(1024)(128)(4,1)S(1)} %get-tuple-element.194, ...), kind=kLoop, calls=%fused_computation.52 | loop fusion | flops 10240 | bytes 14376 | tf_op jit(solution)/shard_map/jit(_take)/select_n | solution.py:143
  114.9 42.5 %all_gather.27 = bf16[32,16,256]{2,1,0:T(8,128)(2,1)} all-gather(bf16[1,16,256]{2,1,0:T(8,128)(2,1)S(1)} %copy-done.5), channel_id=1, replica_groups=mesh['row'=8,'col'=32] {'col'}, dimensions={0}, use_global_device_ids=true | all-gather | bytes 270336 | tf_op jit(solution)/shard_map/all_gather | solution.py:118
  158.4 12.8 %copy.45 = bf16[1024,4608]{1,0:T(8,128)(2,1)} copy(bf16[1024,4608]{0,1:T(8,128)(2,1)} %all-gather.6.cloned.1.call-done) | data formatting | bytes 18874368
  171.2 9.2 %concatenate.11.clone = bf16[1216,4608]{1,0:T(8,128)(2,1)} pad(bf16[1024,4608]{1,0:T(8,128)(2,1)} %copy.45, bf16[]{:T(256)} %constant.176.clone.1), padding=0_192x0_0 | pad | bytes 20643842 | tf_op jit(solution)/shard_map/concatenate | solution.py:69
  180.4 6.0 %fusion.40 = f32[1024,256]{0,1:T(8,128)S(1)} fusion(bf16[1024,4608]{0,1:T(8,128)(2,1)} %all-gather.6.cloned.1.call-done, bf16[4608,256]{1,0:T(8,128)(2,1)} %all-gather.12.cloned.1.call-done), kind=kOutput, calls=%fused_computation.91 | convolution fusion | flops 2415919104 | bytes 12845056 | tf_op jit(solution)/shard_map/dot_general | solution.py:106
  186.8 6.1 %scatter_custom_fusion = bf16[2304,256]{1,0:T(8,128)(2,1)} fusion(s32[1024]{0:T(1024)S(1)} %get-tuple-element.188, bf16[1024,256]{1,0:T(8,128)(2,1)S(1)} %copy.43, bf16[]{:T(256)} %constant.176.clone.1), kind=kCustom, calls=%fused_computation.23 | custom fusion | bytes 1179650 | tf_op jit(solution)/shard_map/scatter | solution.py:153
  192.9 37.9 %all-gather.8.cloned.1.call-done = bf16[4608,512]{1,0:T(8,128)(2,1)} async-done(((bf16[144,512]{1,0:T(8,128)(2,1)}), bf16[4608,512]{1,0:T(8,128)(2,1)}) %all-gather.8.cloned.1.call-update) | async-done | bytes 4718608 | tf_op jit(solution)/shard_map/all_gather | solution.py:103
  230.7 9.1 %fusion.39 = f32[1024,512]{0,1:T(8,128)S(1)} fusion(bf16[1024,4608]{0,1:T(8,128)(2,1)} %all-gather.6.cloned.1.call-done, bf16[4608,512]{1,0:T(8,128)(2,1)} %all-gather.8.cloned.1.call-done), kind=kOutput, calls=%fused_computation.90 | convolution fusion | flops 4831838208 | bytes 16252928 | tf_op jit(solution)/shard_map/dot_general | solution.py:101
  239.8 97.2 %all-gather.10.cloned.1.call-done = bf16[32,4608,32]{1,2,0:T(8,128)(2,1)} async-done(((bf16[1,4608,32]{1,2,0:T(8,128)(2,1)}), bf16[32,4608,32]{1,2,0:T(8,128)(2,1)}) %all-gather.10.cloned.1.call-update) | async-done | bytes 9437200 | tf_op jit(solution)/shard_map/all_gather | solution.py:140
  337.1 91.2 %while.14 = (s32[]{:T(128)}, f32[1216,32]{0,1:T(8,128)S(1)}, s32[10]{0:T(128)S(1)}, bf16[1216,4608]{1,0:T(8,128)(2,1)}, s32[10]{0:T(128)S(1)}, /*index=5*/bf16[3...) while((s32[]{:T(128)}, f32[1216,32]{0,1:T(8,128)S(1)}, ...), condition=%wide.region_3.5_spmd.clone, body=%wide.region_2.4_spmd.clone.sunk | while | flops 56635784 | bytes 2165989 | solution.py:82
  343.4 2.2 fusion.52
  352.4 2.2 fusion.52
  361.5 2.2 fusion.52
  370.6 2.2 fusion.52
  398.0 2.2 fusion.52
  407.2 2.2 fusion.52
  416.3 2.2 fusion.52
  431.4 7.0 %fusion.13 = bf16[1024,256]{1,0:T(8,128)(2,1)S(1)} fusion(f32[1024,256]{1,0:T(8,128)S(1)} %convolution_bitcast_fusion, bf16[1024,4608]{0,1:T(8,128)(2,1)} %all-gather.6.cloned.1.call-done, bf16[4608,256]{1,0:T(8,128)(2,1)} %all-gather.14.cloned.1.call-done), kind=kOutput, calls=%fused_computation.15 | convolution fusion | flops 2416443392 | bytes 13369344 | tf_op jit(solution)/shard_map/dot_general | solution.py:111
  438.5 6.1 %scatter_custom_fusion.1 = bf16[2304,256]{1,0:T(8,128)(2,1)} fusion(s32[1024]{0:T(1024)S(1)} %get-tuple-element.188, bf16[1024,256]{1,0:T(8,128)(2,1)S(1)} %fusion.13, bf16[]{:T(256)} %constant.176.clone.1), kind=kCustom, calls=%fused_computation.21 | custom fusion | bytes 1179650 | tf_op jit(solution)/shard_map/scatter | solution.py:159
  (131 shorter events, 61.6 us)
Async XLA Ops:
  7.2 67.3 %copy-start = (s32[32]{0:T(128)S(1)}, s32[32]{0:T(128)}, u32[]{:S(2)}) copy-start(s32[32]{0:T(128)} %param.24) | copy-start | bytes 388
  7.2 22.5 %copy-start.4 = (bf16[1,16,512]{2,1,0:T(8,128)(2,1)S(1)}, bf16[1,16,512]{2,1,0:T(8,128)(2,1)}, u32[]{:S(2)}) copy-start(bf16[1,16,512]{2,1,0:T(8,128)(2,1)} %param.20) | copy-start | bytes 49156
  7.2 66.8 %copy-start.6 = (s32[1,10]{1,0:T(1,128)S(1)}, s32[1,10]{1,0:T(1,128)}, u32[]{:S(2)}) copy-start(s32[1,10]{1,0:T(1,128)} %param.22) | copy-start | bytes 124
  7.2 67.2 %copy-start.7 = (s32[1,10]{1,0:T(1,128)S(1)}, s32[1,10]{1,0:T(1,128)}, u32[]{:S(2)}) copy-start(s32[1,10]{1,0:T(1,128)} %param.23) | copy-start | bytes 124
  7.2 69.3 %copy-start.3 = (s32[1,18]{1,0:T(1,128)S(1)}, s32[1,18]{1,0:T(1,128)}, u32[]{:S(2)}) copy-start(s32[1,18]{1,0:T(1,128)} %param.25) | copy-start | bytes 220
  7.2 107.6 %copy-start.5 = (bf16[1,16,256]{2,1,0:T(8,128)(2,1)S(1)}, bf16[1,16,256]{2,1,0:T(8,128)(2,1)}, u32[]{:S(2)}) copy-start(bf16[1,16,256]{2,1,0:T(8,128)(2,1)} %param.21) | copy-start | bytes 24580
  7.2 151.1 %all-gather.6.cloned.1.call-start = ((), (), s32[]{:S(2)}) async-start(), calls=%async_computation | async-start | bytes 10616832 | tf_op jit(solution)/shard_map/all_gather | solution.py:100
  8.0 172.4 %all-gather.12.cloned.1.call-start = ((), (), s32[]{:S(2)}) async-start(), calls=%async_computation.3 | async-start | bytes 2433024 | tf_op jit(solution)/shard_map/all_gather | solution.py:108
  8.7 222.0 %all-gather.8.cloned.1.call-start = ((), (), s32[]{:S(2)}) async-start(), calls=%async_computation.1 | async-start | bytes 4866048 | tf_op jit(solution)/shard_map/all_gather | solution.py:103
  9.4 327.6 %all-gather.10.cloned.1.call-start = ((), (), s32[]{:S(2)}) async-start(), calls=%async_computation.2 | async-start | bytes 9732096 | tf_op jit(solution)/shard_map/all_gather | solution.py:140
  9.5 4.1 collective-permute-start
  12.2 3.6 collective-permute-start.1
  13.6 4.6 %collective-permute-start.2 = (bf16[1,576,32]{1,2,0:T(8,128)(2,1)S(1)}, bf16[1,576,32]{1,2,0:T(8,128)(2,1)S(1)}, u32[]{:S(2)}, u32[]{:S(2)}) collective-permute-start(bf16[1,576,32]{1,2,0:T(8,128)(2,1)S(1)} %collective-permute-done), channel_id=1, source_target_pairs={{0,32},{32,64},{64,96},{96,128},{128,160},{160,192},{192,224},{224... | collective-permute-start | bytes 110600 | tf_op jit(solution)/shard_map/ppermute | solution.py:131
  15.8 3.4 collective-permute-start.3
  18.3 4.6 %collective-permute-start.4 = (bf16[1,576,32]{1,2,0:T(8,128)(2,1)S(1)}, bf16[1,576,32]{1,2,0:T(8,128)(2,1)S(1)}, u32[]{:S(2)}, u32[]{:S(2)}) collective-permute-start(bf16[1,576,32]{1,2,0:T(8,128)(2,1)S(1)} %collective-permute-done.2), channel_id=1, source_target_pairs={{0,32},{32,64},{64,96},{96,128},{128,160},{160,192},{192,224},{224... | collective-permute-start | bytes 110600 | tf_op jit(solution)/shard_map/ppermute | solution.py:131
  19.3 7.8 %collective-permute-start.5 = (bf16[1,576,32]{1,2,0:T(8,128)(2,1)S(1)}, bf16[1,576,32]{1,2,0:T(8,128)(2,1)S(1)}, u32[]{:S(2)}, u32[]{:S(2)}) collective-permute-start(bf16[1,576,32]{1,2,0:T(8,128)(2,1)S(1)} %collective-permute-done.3), channel_id=1, source_target_pairs={{0,224},{32,0},{64,32},{96,64},{128,96},{160,128},{192,160},{224,1... | collective-permute-start | bytes 110600 | tf_op jit(solution)/shard_map/ppermute | solution.py:136
  22.9 4.7 %collective-permute-start.6 = (bf16[1,576,32]{1,2,0:T(8,128)(2,1)S(1)}, bf16[1,576,32]{1,2,0:T(8,128)(2,1)S(1)}, u32[]{:S(2)}, u32[]{:S(2)}) collective-permute-start(bf16[1,576,32]{1,2,0:T(8,128)(2,1)S(1)} %collective-permute-done.4), channel_id=1, source_target_pairs={{0,32},{32,64},{64,96},{96,128},{128,160},{160,192},{192,224},{224... | collective-permute-start | bytes 110600 | tf_op jit(solution)/shard_map/ppermute | solution.py:131
  28.3 0.7 copy-start.1
  29.0 402.4 %all-gather.14.cloned.1.call-start = ((), (), s32[]{:S(2)}) async-start(), calls=%async_computation.4 | async-start | bytes 2433024 | tf_op jit(solution)/shard_map/all_gather | solution.py:113
  429.5 1.4 copy-start.2
Sparse Core Ops, SparseCore 0:
  9.9 61.0 all-gather.5
  73.6 73.6 all-gather.11
  149.9 80.8 all-gather.7
  233.8 103.2 all-gather.9
  339.5 71.4 all-gather.13
